TPU v7x, 256 devices: a whole 4x4x8 slice. The times are simulated.
256 devices in a mesh: seq: 16 (over z, core), head: 16 (over x, y).
Axes of the slice: x: 4, y: 4, z: 8, core: 2. Of those that a mesh axis runs over, the one named last changes fastest.
Arguments:
- hidden_in: bfloat16 [4, 128, 2048], P(None, None, 'seq'), may hold values from -6 to 6
- attn_gain: float32 [2048], P('seq'), may hold values from 0.1 to 1.9
- attn_router: bfloat16 [2048, 8], P('seq'), may hold values from -0.125 to 0.125
- query_weight: bfloat16 [2048, 8, 2048], P('seq', None, 'head'), may hold values from -0.125 to 0.125
- kv_weight: bfloat16 [2048, 4096], P('seq', 'head'), may hold values from -0.125 to 0.125
- out_weight: bfloat16 [8, 2048, 2048], P(None, 'head', 'seq'), may hold values from -0.09375 to 0.09375
- mlp_gain: float32 [2048], replicated, may hold values from 0.1 to 1.9
- mlp_router: bfloat16 [2048, 8], replicated, may hold values from -0.125 to 0.125
- gate_weight: bfloat16 [2048, 45056], P(None, ('seq', 'head')), may hold values from -0.125 to 0.125
- up_weight: bfloat16 [2048, 45056], P(None, ('seq', 'head')), may hold values from -0.125 to 0.125
- down_weight: bfloat16 [45056, 2048], P(('seq', 'head')), may hold values from -0.3125 to 0.3125
- cache: bfloat16 [196608, 4096], P('seq', 'head'), as said below
- token_req: int32 [196608], P('seq'), may hold values from -1 to 127, as said below
- attn_route: int32 [4, 128, 2], replicated, may hold values from 0 to 7, all different within a row
- mlp_route: int32 [4, 128, 2], replicated, may hold values from 0 to 7, all different within a row; in each aligned block of 512 rows (0 to 511, 512 to 1023, ..., all dimensions but the last counted through in order) at most 192 rows name the same one
- owner: int32 [128], replicated, may hold values from 0 to 15, as said below
Outputs:
- hidden_out: bfloat16 [4, 128, 2048], P(None, 'head', 'seq')
- new_cache: bfloat16 [160, 4, 4096], P('seq', None, 'head')
Inputs may be any that keep to these rules, and one draw needn't show every extreme that they name: `token_req`: slots form pages of 128; the live slots of a page belong to one request; request r has lengths[r] live slots; four requests have exactly 32768, every other at least one and less than 512. At most 10 requests share an owner, and some owner has exactly 10. `cache`: rows of empty slots hold values too. `attn_route`: the 2 experts of a token differ. `mlp_route`: the 2 experts of a token differ; over all 4 x 128 tokens no expert is chosen more than 192 times, and one is chosen exactly 192 times.
All inputs are finite; a program needn't handle non-finite values.
Results may differ from a plain program's by a relative error of at most 0.019.
Values may be sent and summed in bfloat16 or wider, within the bound.
No kernel may reach another device: no remote copies, remote signals or barrier semaphores. Data moves between devices by JAX's collectives and lax.ppermute only.
A program may use at most 64 MiB of HBM per device.

v0:
```python
import math
import jax
import jax.numpy as jnp
from jax import lax
from jax.sharding import PartitionSpec as P

D = 2048
HD = 128
FF = 5632
PAGE = 128
OWN_MAX = 10
epsilon = 1e-06
masked_score = -1e30


def frequency(width):
    return jnp.power(jnp.float32(10000.0), -2.0 * jnp.arange(width // 2, dtype=jnp.float32) / width)


def rotate(values, angles):
    half_width = values.shape[-1] // 2
    cosine = jnp.cos(angles)
    sine_part = jnp.sin(angles)
    lower_half = values[..., :half_width]
    upper_half = values[..., half_width:]
    return jnp.concatenate(
        [
            lower_half * cosine - upper_half * sine_part,
            upper_half * cosine + lower_half * sine_part,
        ],
        axis=-1,
    )


def on_device(
    hidden_in,
    attn_gain,
    attn_router,
    query_weight,
    kv_weight,
    out_weight,
    mlp_gain,
    mlp_router,
    gate_weight,
    up_weight,
    down_weight,
    cache,
    token_req,
    attn_route,
    mlp_route,
    owner,
):
    highest = lax.Precision.HIGHEST
    step_count, req_count, local_width = hidden_in.shape
    head_count = lax.axis_size("head")
    seq_index = lax.axis_index("seq")
    head_index = lax.axis_index("head")
    experts = query_weight.shape[1]
    heads_dev = kv_weight.shape[1] // (2 * HD)
    top_count = attn_route.shape[2]
    tok_rows = step_count * req_count
    queries_all = step_count * top_count
    hidden_f = hidden_in.astype(jnp.float32)
    squares = jnp.sum(hidden_f * hidden_f, axis=2)
    scaled = (hidden_f * attn_gain).astype(jnp.bfloat16).reshape(tok_rows, local_width)
    query_part = jnp.dot(
        scaled,
        query_weight.reshape(local_width, experts * heads_dev * HD),
        preferred_element_type=jnp.float32,
    ).reshape(step_count, req_count, experts, heads_dev * HD)
    kv_part = jnp.dot(scaled, kv_weight, preferred_element_type=jnp.float32).reshape(
        step_count, req_count, heads_dev * 2 * HD
    )
    logit_part = jnp.dot(scaled, attn_router, preferred_element_type=jnp.float32).reshape(
        step_count, req_count, experts
    )
    request_ids = jnp.arange(req_count, dtype=jnp.int32)
    counts = jnp.sum((token_req[:, None] == request_ids[None, :]).astype(jnp.float32), axis=0)
    attn_hot = (attn_route[..., None] == jnp.arange(experts, dtype=jnp.int32)).astype(jnp.float32)
    query_sum, kv_sum, logit_sum, square_sum, lengths = lax.psum(
        (query_part, kv_part, logit_part, squares, counts), "seq"
    )
    picked = jnp.einsum("srke,srec->srkc", attn_hot, query_sum, precision=highest)
    inverse = lax.rsqrt(square_sum / D + epsilon)
    attn_gates = jax.nn.softmax(
        jnp.sum(attn_hot * (logit_sum * inverse[..., None])[:, :, None, :], axis=3), axis=2
    )
    positions = lengths[None, :] + jnp.arange(step_count, dtype=jnp.float32)[:, None]
    freq_table = frequency(HD)
    queries = (picked * inverse[..., None, None]).reshape(
        step_count, req_count, top_count, heads_dev, HD
    )
    queries = rotate(queries, positions[:, :, None, None, None] * freq_table).astype(jnp.bfloat16)
    projected = kv_sum.reshape(step_count, req_count, heads_dev, 2 * HD) * inverse[..., None, None]
    new_keys = rotate(projected[..., :HD], positions[:, :, None, None] * freq_table).astype(
        jnp.bfloat16
    )
    new_values = projected[..., HD:].astype(jnp.bfloat16)
    new_rows = jnp.concatenate([new_keys, new_values], axis=3).reshape(
        step_count, req_count, heads_dev * 2 * HD
    )
    owned_flag = (owner == seq_index).astype(jnp.int32)
    before = (request_ids[None, :] < request_ids[:, None]).astype(jnp.int32)
    slot_rank = jnp.sum(before * owned_flag[None, :], axis=1)
    slot_ids = jnp.arange(OWN_MAX, dtype=jnp.int32)
    select = ((owned_flag[None, :] == 1) & (slot_rank[None, :] == slot_ids[:, None])).astype(
        jnp.bfloat16
    )
    appended = jnp.einsum(
        "jr,src->jsc", select, new_rows, preferred_element_type=jnp.float32
    ).astype(jnp.bfloat16)
    page_total = token_req.shape[0] // PAGE
    page_owner = token_req.reshape(page_total, PAGE)
    page_req = jnp.max(page_owner, axis=1)
    page_pick = jnp.maximum(page_req, 0)
    live_slot = page_owner >= 0
    req_hot = (page_req[None, :] == request_ids[:, None]).astype(jnp.float32)
    query_rows = jnp.transpose(queries, (1, 3, 0, 2, 4)).reshape(
        req_count, heads_dev, queries_all, HD
    )
    page_queries = query_rows[page_pick]
    paged = cache.reshape(page_total, PAGE, heads_dev, 2 * HD)
    score_scale = 1.0 / math.sqrt(HD)
    scores = (
        jnp.einsum(
            "phqd,pthd->phqt", page_queries, paged[..., :HD], preferred_element_type=jnp.float32
        )
        * score_scale
    )
    scores = jnp.where(live_slot[:, None, None, :], scores, masked_score)
    fresh_keys = jnp.transpose(new_keys, (1, 2, 0, 3))
    fresh_values = jnp.transpose(new_values, (1, 2, 0, 3))
    fresh_scores = (
        jnp.einsum("rhqd,rhsd->rhqs", query_rows, fresh_keys, preferred_element_type=jnp.float32)
        * score_scale
    )
    query_step = jnp.arange(queries_all) // top_count
    causal = jnp.arange(step_count)[None, :] <= query_step[:, None]
    fresh_live = causal[None, None, :, :] & (owned_flag[:, None, None, None] == 1)
    fresh_scores = jnp.where(fresh_live, fresh_scores, masked_score)
    page_best = jnp.max(scores, axis=3)
    local_best = jnp.max(
        jnp.where(req_hot[:, :, None, None] > 0, page_best[None], masked_score), axis=1
    )
    local_best = jnp.maximum(local_best, jnp.max(fresh_scores, axis=3))
    maxima = lax.pmax(local_best, "seq")
    page_probs = jnp.where(
        live_slot[:, None, None, :], jnp.exp(scores - maxima[page_pick][..., None]), 0.0
    )
    page_sums = jnp.sum(page_probs, axis=3)
    page_out = jnp.einsum(
        "phqt,pthd->phqd",
        page_probs.astype(jnp.bfloat16),
        paged[..., HD:],
        preferred_element_type=jnp.float32,
    )
    fresh_probs = jnp.where(fresh_live, jnp.exp(fresh_scores - maxima[..., None]), 0.0)
    totals = jnp.einsum("rp,phq->rhq", req_hot, page_sums, precision=highest) + jnp.sum(
        fresh_probs, axis=3
    )
    outputs = jnp.einsum("rp,phqd->rhqd", req_hot, page_out, precision=highest)
    outputs = outputs + jnp.einsum(
        "rhqs,rhsd->rhqd",
        fresh_probs.astype(jnp.bfloat16),
        fresh_values,
        preferred_element_type=jnp.float32,
    )
    local_totals = totals
    local_outputs = outputs
    totals, outputs = (
        lax.psum(local_totals.astype(jnp.bfloat16), "seq").astype(jnp.float32),
        lax.psum(local_outputs.astype(jnp.bfloat16), "seq").astype(jnp.float32),
    )
    attention = outputs / totals[..., None]
    attention = jnp.transpose(
        attention.reshape(req_count, heads_dev, step_count, top_count, HD), (2, 0, 3, 1, 4)
    )
    weighted = (attention * attn_gates[..., None, None]).astype(jnp.bfloat16)
    mixed = jnp.einsum(
        "srkhd,srke->srehd", weighted.astype(jnp.float32), attn_hot, precision=highest
    ).astype(jnp.bfloat16)
    head_part = jnp.dot(
        mixed.reshape(tok_rows, experts * heads_dev * HD),
        out_weight.reshape(experts * heads_dev * HD, local_width),
        preferred_element_type=jnp.float32,
    ).reshape(step_count, req_count, local_width)
    attn_out = lax.psum(head_part.astype(jnp.bfloat16), "head").astype(jnp.float32)
    residual = (hidden_f + attn_out).astype(jnp.bfloat16)
    full_rows = lax.all_gather(residual, "seq", axis=2, tiled=True)
    full_f = full_rows.astype(jnp.float32)
    inverse_mlp = lax.rsqrt(jnp.mean(full_f * full_f, axis=2) + epsilon)
    normed = (full_f * inverse_mlp[..., None] * mlp_gain).astype(jnp.bfloat16).reshape(tok_rows, D)
    mlp_logits = jnp.dot(normed, mlp_router, preferred_element_type=jnp.float32).reshape(
        step_count, req_count, experts
    )
    mlp_hot = (mlp_route[..., None] == jnp.arange(experts, dtype=jnp.int32)).astype(jnp.float32)
    mlp_gates = jax.nn.softmax(jnp.sum(mlp_hot * mlp_logits[:, :, None, :], axis=3), axis=2)
    combine_w = jnp.sum(mlp_hot * mlp_gates[..., None], axis=2)
    unit_count = gate_weight.shape[1]
    device_index = seq_index * head_count + head_index
    expert_index = device_index * unit_count // FF
    expert_ids = jnp.arange(experts, dtype=jnp.int32)
    rows_dev = req_count // head_count
    expert_weight = jnp.sum(
        combine_w * (expert_ids == expert_index).astype(jnp.float32), axis=2
    ).reshape(tok_rows, 1)
    gate_pre = jnp.dot(normed, gate_weight, preferred_element_type=jnp.float32)
    up_pre = jnp.dot(normed, up_weight, preferred_element_type=jnp.float32)
    hidden_units = (jax.nn.silu(gate_pre) * up_pre).astype(jnp.bfloat16)
    expert_term = (
        jnp.dot(hidden_units, down_weight, preferred_element_type=jnp.float32) * expert_weight
    ).reshape(step_count, req_count, D)
    by_columns = lax.psum_scatter(
        expert_term.astype(jnp.bfloat16), "seq", scatter_dimension=2, tiled=True
    )
    expert_part = lax.psum_scatter(by_columns, "head", scatter_dimension=1, tiled=True).astype(
        jnp.float32
    )
    own_rows = lax.dynamic_slice_in_dim(residual, head_index * rows_dev, rows_dev, 1)
    hidden_out = (own_rows.astype(jnp.float32) + expert_part).astype(jnp.bfloat16)
    return (hidden_out, appended)


def solution(mesh):
    in_specs = (
        P(None, None, "seq"),
        P("seq"),
        P("seq", None),
        P("seq", None, "head"),
        P("seq", "head"),
        P(None, "head", "seq"),
        P(),
        P(),
        P(None, ("seq", "head")),
        P(None, ("seq", "head")),
        P(("seq", "head"), None),
        P("seq", "head"),
        P("seq"),
        P(),
        P(),
        P(),
    )
    out_specs = (P(None, "head", "seq"), P("seq", None, "head"))
    return jax.shard_map(
        on_device, mesh=mesh, in_specs=in_specs, out_specs=out_specs, check_vma=False
    )
```

profile of v0, /device:TPU:2, one launch (start us, length us, event | category | flops | bytes accessed | tf_op | source)
XLA Modules:
  0.0 634.6 jit_solution(8452154288114500692)
XLA Ops:
  7.2 1.1 copy.167
  8.5 2.0 fusion.79
  10.4 2.7 fusion.67
  13.4 5.5 convert_reduce_fusion
  19.2 50.9 %all-reduce.1 = (f32[4,128]{1,0:T(4,128)S(1)}, f32[128]{0:T(128)S(1)}, f32[4,128,8]{1,2,0:T(8,128)S(1)}) all-reduce(f32[4,128]{1,0:T(4,128)S(1)} %fusion.46, f32[128]{0:T(128)S(1)} %convert_reduce_fusion, f32[4,128,8]{1,2,0:T(8,128)S(1)} %fusion.77), channel_id=1, replica_groups=mesh['seq'=16,'head'=16] {'seq'}, use_global_device_ids=true, to_apply=%region_3.0 | all-reduce | flops 4736 | bytes 37888 | tf_op jit(solution)/shard_map/psum | solution.py:80
  70.6 7.3 %select_reduce_fusion.2 = f32[4,128,2]{2,1,0:T(8,128)S(1)} fusion(f32[4,128,8]{2,1,0:T(8,128)S(1)} %copy.124, s32[4,128,2]{2,1,0:T(8,128)S(1)} %copy.111), kind=kLoop, calls=%fused_computation.46 | loop fusion | flops 23552 | bytes 24576 | tf_op jit(solution)/shard_map/reduce_sum | solution.py:86
  77.8 0.8 fusion.103
  78.8 1.0 multiply_cosine_fusion.1
  79.8 53.4 %all-reduce.14.cloned.1.call-done = (f32[4,128,256]{2,1,0:T(8,128)}, f32[4,128,8,128]{3,1,2,0:T(8,128)}) async-done(((f32[4,128,256]{2,1,0:T(8,128)}, f32[4,128,8,128]{3,1,2,0:T(8,128)}), (f32[4,128,256]{2,1,0:T(8,128)}, f32[4,128,8,128]{3,1,2,0:T(8,128)})) %all-reduce.14.cloned.1.call-update) | async-done | bytes 2621456 | tf_op jit(solution)/shard_map/psum | solution.py:80
  133.2 1.3 multiply_bitcast_fusion
  134.5 1.2 fusion.42
  135.8 3.2 fusion.12
  138.9 0.8 subtract_convert_fusion
  139.8 0.7 maximum_bitcast_fusion
  140.7 0.7 gather_fusion
  141.4 3.7 fusion.101
  145.5 0.5 fusion.102
  146.0 48.3 %pmax.7 = f32[128,1,8]{2,0,1:T(8,128)S(1)} all-reduce(f32[128,1,8]{2,0,1:T(8,128)S(1)} %maximum_bitcast_fusion.4), channel_id=1, replica_groups=mesh['seq'=16,'head'=16] {'seq'}, use_global_device_ids=true, to_apply=%region_10.0 | all-reduce | flops 1024 | bytes 8192 | tf_op jit(solution)/shard_map/pmax | solution.py:146
  194.3 0.6 gather_fusion.1
  194.9 2.9 fusion.5
  198.4 0.7 fusion.65
  199.1 1.3 fusion.21
  200.7 23.6 %psum.61 = bf16[128,8]{0,1:T(8,128)(2,1)S(1)} all-reduce(bf16[128,8]{0,1:T(8,128)(2,1)S(1)} %fusion.26), channel_id=1, replica_groups=mesh['seq'=16,'head'=16] {'seq'}, use_global_device_ids=true, to_apply=%region_14.15 | all-reduce | flops 1024 | bytes 4096 | tf_op jit(solution)/shard_map/psum | solution.py:171
  224.3 83.3 %all-reduce.8.cloned.1.call-done = bf16[128,1,8,128]{3,0,2,1:T(8,128)(2,1)} async-done(((bf16[128,1,8,128]{3,0,2,1:T(8,128)(2,1)}), bf16[128,1,8,128]{3,0,2,1:T(8,128)(2,1)}) %all-reduce.8.cloned.1.call-update) | async-done | bytes 262160 | tf_op jit(solution)/shard_map/psum | solution.py:172
  307.6 1.2 convert_divide_fusion
  308.8 2.7 convolution_convert_fusion
  311.6 1.1 fusion.25
  312.7 92.5 %all-reduce.10.cloned.1.call-done = bf16[4,128,128]{2,1,0:T(8,128)(2,1)} async-done(((bf16[4,128,128]{2,1,0:T(8,128)(2,1)}), bf16[4,128,128]{2,1,0:T(8,128)(2,1)}) %all-reduce.10.cloned.1.call-update) | async-done | bytes 131088 | tf_op jit(solution)/shard_map/psum | solution.py:187
  405.2 1.6 fusion.47
  407.1 40.6 %all-gather.2.cloned.1.call-done = bf16[4,128,2048]{2,1,0:T(8,128)(2,1)} async-done(((bf16[4,128,128]{2,1,0:T(8,128)(2,1)}), bf16[4,128,2048]{2,1,0:T(8,128)(2,1)}) %all-gather.2.cloned.1.call-update) | async-done | bytes 2097168 | tf_op jit(solution)/shard_map/all_gather | solution.py:189
  447.7 2.2 fusion.2
  450.0 0.5 fusion.4
  450.5 1.3 copy-done.2
  451.9 0.7 fusion.85
  452.6 7.3 %select_reduce_fusion.1 = f32[4,128,2]{2,1,0:T(8,128)S(1)} fusion(f32[4,128,8]{2,1,0:T(8,128)S(1)} %fusion.85, s32[4,128,2]{2,1,0:T(8,128)S(1)} %copy.126), kind=kLoop, calls=%fused_computation.44 | loop fusion | flops 23552 | bytes 24576 | tf_op jit(solution)/shard_map/reduce_sum | solution.py:197
  460.1 1.4 select_reduce_fusion
  461.7 3.5 fusion.104
  465.2 4.1 multiply_convert_fusion
  469.4 3.1 copy.133
  472.5 1.7 copy.166
  474.3 0.6 copy-done.17
  474.9 0.6 dynamic-slice
  476.2 56.6 %reduce-scatter.5.cloned.1.call-done = bf16[128,512]{1,0:T(8,128)(2,1)} async-done(((bf16[2048,512]{1,0:T(8,128)(2,1)}), bf16[128,512]{1,0:T(8,128)(2,1)}) %reduce-scatter.5.cloned.1.call-update) | async-done | bytes 131088
  532.9 0.9 reshape.447
  533.8 0.8 copy.134
  534.9 0.6 copy.129
  535.5 91.0 %all-reduce.12.cloned.1.call-done = bf16[4,128,128]{2,1,0:T(8,128)(2,1)} async-done(((bf16[4,128,128]{2,1,0:T(8,128)(2,1)}), bf16[4,128,128]{2,1,0:T(8,128)(2,1)}) %all-reduce.12.cloned.1.call-update) | async-done | bytes 131088
  626.5 1.3 add_convert_fusion.1
  (84 shorter events, 4.1 us)
Async XLA Ops:
  7.2 458.1 %copy-start = (bf16[176,2048]{1,0:T(8,128)(2,1)S(1)}, bf16[176,2048]{1,0:T(8,128)(2,1)}, u32[]{:S(2)}) copy-start(bf16[176,2048]{1,0:T(8,128)(2,1)} %param.26) | copy-start | bytes 2162692
  7.2 126.0 %all-reduce.14.cloned.1.call-start = ((), (), s32[]{:S(2)}) async-start(), calls=%async_computation.6 | async-start | bytes 5242880 | tf_op jit(solution)/shard_map/psum | solution.py:80
  10.4 2.8 copy-start.4
  10.4 3.0 copy-start.7
  10.4 8.7 %copy-start.11 = (f32[128]{0:T(128)S(1)}, f32[128]{0:T(128)}, u32[]{:S(2)}) copy-start(f32[128]{0:T(128)} %param.17) | copy-start | bytes 1540
  10.4 8.7 %copy-start.16 = (bf16[128,8]{0,1:T(8,128)(2,1)S(1)}, bf16[128,8]{0,1:T(8,128)(2,1)}, u32[]{:S(2)}) copy-start(bf16[128,8]{0,1:T(8,128)(2,1)} %param.18) | copy-start | bytes 6148
  13.1 57.1 %copy-start.12 = (s32[128]{0:T(128)S(1)}, s32[128]{0:T(128)}, u32[]{:S(2)}) copy-start(s32[128]{0:T(128)} %param.31) | copy-start | bytes 1540
  13.1 57.1 %copy-start.9 = (s32[4,128,2]{1,2,0:T(2,128)S(1)}, s32[4,128,2]{1,2,0:T(2,128)}, u32[]{:S(2)}) copy-start(s32[4,128,2]{1,2,0:T(2,128)} %param.29) | copy-start | bytes 12292
  13.2 294.5 %all-reduce.8.cloned.1.call-start = ((), (), s32[]{:S(2)}) async-start(), calls=%async_computation.1 | async-start | bytes 524288 | tf_op jit(solution)/shard_map/psum | solution.py:172
  133.2 2.6 copy-start.13
  135.7 9.7 %copy-start.5 = (bf16[4,128,1,64]{3,1,0,2:T(8,128)(2,1)}, bf16[4,128,1,64]{3,1,0,2:T(8,128)(2,1)S(1)}, u32[]{:S(2)}) copy-start(bf16[4,128,1,64]{3,1,0,2:T(8,128)(2,1)S(1)} %get-tuple-element.26) | copy-start | bytes 196612
  200.4 204.9 %all-reduce.10.cloned.1.call-start = ((), (), s32[]{:S(2)}) async-start(), calls=%async_computation.2 | async-start | bytes 262144 | tf_op jit(solution)/shard_map/psum | solution.py:187
  308.8 2.7 copy-start.14
  311.5 95.4 %copy-start.10 = (s32[4,128,2]{1,2,0:T(2,128)S(1)}, s32[4,128,2]{1,2,0:T(2,128)}, u32[]{:S(2)}) copy-start(s32[4,128,2]{1,2,0:T(2,128)} %param.30) | copy-start | bytes 12292
  311.6 138.4 %copy-start.8 = (f32[2048]{0:T(1024)S(1)}, f32[2048]{0:T(1024)}, u32[]{:S(2)}) copy-start(f32[2048]{0:T(1024)} %param.22) | copy-start | bytes 24580
  312.7 135.0 %all-gather.2.cloned.1.call-start = ((), (), s32[]{:S(2)}) async-start(), calls=%async_computation.3 | async-start | bytes 2228224 | tf_op jit(solution)/shard_map/all_gather | solution.py:189
  406.8 126.0 %reduce-scatter.5.cloned.1.call-start = ((), (), s32[]{:S(2)}) async-start(), calls=%async_computation.4 | async-start | bytes 2228224
  447.7 2.2 copy-start.1
  450.0 1.9 copy-start.15
  450.5 1.4 copy-start.2
  461.7 3.5 copy-start.3
  474.2 0.7 copy-start.17
  474.2 60.4 %copy-start.6 = (bf16[4,128,1,64]{3,1,0,2:T(8,128)(2,1)S(1)}, bf16[4,128,1,64]{3,1,0,2:T(8,128)(2,1)}, u32[]{:S(2)}) copy-start(bf16[4,128,1,64]{3,1,0,2:T(8,128)(2,1)} %copy-done.5) | copy-start | bytes 196612
  474.2 152.2 %all-reduce.12.cloned.1.call-start = ((), (), s32[]{:S(2)}) async-start(), calls=%async_computation.5 | async-start | bytes 262144
Sparse Core Ops, SparseCore 0:
  13.3 119.8 all-reduce.13
  200.5 107.0 all-reduce.7
  312.8 92.3 all-reduce.9
  407.0 40.6 all-gather.1
  474.3 58.4 reduce-scatter.4
  535.9 90.5 all-reduce.11
where the time goes:
time: 635 us
  waiting for transfers between devices  418 us (66%)
  blocking collectives  123 us (19%)
  other arithmetic  36 us (6%)
  matrix products  29.6 us (5%)
  between operations  15.3 us (2%)
  local copies, waits for them, and re-layouts  13.2 us (2%)
    unnamed x8, waiting for transfers between devices  148 us
    psum x1, waiting for transfers between devices, on_device(): lax.psum(head_part.astype(jnp.bfloat16), 'head').astype(jnp.float32)  92.5 us
    psum x1, waiting for transfers between devices, on_device(): lax.psum(local_outputs.astype(jnp.bfloat16), 'seq').astype(jnp.float32)  83.3 us
    psum x1, waiting for transfers between devices, on_device(): lax.psum((query_part, kv_part, logit_part, squares, counts), 'seq')  53.4 us
    psum x1, blocking collectives, on_device(): lax.psum((query_part, kv_part, logit_part, squares, counts), 'seq')  50.9 us
    pmax x1, blocking collectives, on_device(): maxima = lax.pmax(local_best, 'seq')  48.3 us
    all_gather x1, waiting for transfers between devices, on_device(): full_rows = lax.all_gather(residual, 'seq', axis=2, tiled=True)  40.6 us
    psum x1, blocking collectives, on_device(): lax.psum(local_totals.astype(jnp.bfloat16), 'seq').astype(jnp.float32)  23.6 us
  transfers between devices with their start and end apart: 6, of which 6 were waited for; matrix products, arithmetic and copies ran while one was open for 3% of the time, Pallas kernels for 0%

commit v1 on v0

--- a/solution.py
+++ b/solution.py
@@ -11,6 +11,12 @@
 OWN_MAX = 10
 epsilon = 1e-06
 masked_score = -1e30
+
+
+def add_all(array, axis):
+    pieces = lax.all_gather(array, axis, axis=0, tiled=False)
+    summed = pieces.sum(axis=0)
+    return summed
 
 
 def frequency(width):
@@ -168,7 +174,7 @@
     local_totals = totals
     local_outputs = outputs
     totals, outputs = (
-        lax.psum(local_totals.astype(jnp.bfloat16), "seq").astype(jnp.float32),
+        add_all(local_totals.astype(jnp.bfloat16), "seq").astype(jnp.float32),
         lax.psum(local_outputs.astype(jnp.bfloat16), "seq").astype(jnp.float32),
     )
     attention = outputs / totals[..., None]

time: 635 us -> 635 us (level)
  blocking collectives: 123 us -> 113 us
  waiting for transfers between devices: 418 us -> 427 us
    psum x1 -> x0, blocking collectives: 23.6 us -> none  [on_device(): lax.psum(local_totals.astype(jnp.bfloat16), 'seq').astype(jnp.float32)]
    all_gather x0 -> x1, blocking collectives: none -> 14.2 us  [add_all(): pieces = lax.all_gather(array, axis, axis=0, tiled=False)]
    psum x1, waiting for transfers between devices: 83.3 us -> 92.7 us  [on_device(): lax.psum(local_outputs.astype(jnp.bfloat16), 'seq').astype(jnp.float32)]
where the time goes in v1:
time: 635 us
  waiting for transfers between devices  427 us (67%)
  blocking collectives  113 us (18%)
  other arithmetic  36 us (6%)
  matrix products  29.6 us (5%)
  between operations  15.3 us (2%)
  local copies, waits for them, and re-layouts  13.2 us (2%)
    unnamed x8, waiting for transfers between devices  148 us
    psum x1, waiting for transfers between devices, on_device(): lax.psum(local_outputs.astype(jnp.bfloat16), 'seq').astype(jnp.float32)  92.7 us
    psum x1, waiting for transfers between devices, on_device(): lax.psum(head_part.astype(jnp.bfloat16), 'head').astype(jnp.float32)  92.5 us
    psum x1, waiting for transfers between devices, on_device(): lax.psum((query_part, kv_part, logit_part, squares, counts), 'seq')  53.4 us
    psum x1, blocking collectives, on_device(): lax.psum((query_part, kv_part, logit_part, squares, counts), 'seq')  50.9 us
    pmax x1, blocking collectives, on_device(): maxima = lax.pmax(local_best, 'seq')  48.3 us
    all_gather x1, waiting for transfers between devices, on_device(): full_rows = lax.all_gather(residual, 'seq', axis=2, tiled=True)  40.6 us
    all_gather x1, blocking collectives, add_all(): pieces = lax.all_gather(array, axis, axis=0, tiled=False)  14.2 us
  transfers between devices with their start and end apart: 6, of which 6 were waited for; matrix products, arithmetic and copies ran while one was open for 3% of the time, Pallas kernels for 0%

profile of v1, /device:TPU:2, one launch (start us, length us, event | category | flops | bytes accessed | tf_op | source)
XLA Modules:
  0.0 634.6 jit_solution(17667059466848687357)
XLA Ops:
  7.2 1.1 copy.167
  8.5 2.0 fusion.79
  10.4 2.7 fusion.67
  13.4 5.5 convert_reduce_fusion
  19.2 50.9 %all-reduce.1 = (f32[4,128]{1,0:T(4,128)S(1)}, f32[128]{0:T(128)S(1)}, f32[4,128,8]{1,2,0:T(8,128)S(1)}) all-reduce(f32[4,128]{1,0:T(4,128)S(1)} %fusion.46, f32[128]{0:T(128)S(1)} %convert_reduce_fusion, f32[4,128,8]{1,2,0:T(8,128)S(1)} %fusion.77), channel_id=1, replica_groups=mesh['seq'=16,'head'=16] {'seq'}, use_global_device_ids=true, to_apply=%region_3.0 | all-reduce | flops 4736 | bytes 37888 | tf_op jit(solution)/shard_map/psum | solution.py:86
  70.6 7.3 %select_reduce_fusion.2 = f32[4,128,2]{2,1,0:T(8,128)S(1)} fusion(f32[4,128,8]{2,1,0:T(8,128)S(1)} %copy.124, s32[4,128,2]{2,1,0:T(8,128)S(1)} %copy.111), kind=kLoop, calls=%fused_computation.46 | loop fusion | flops 23552 | bytes 24576 | tf_op jit(solution)/shard_map/reduce_sum | solution.py:92
  77.8 0.8 fusion.103
  78.8 1.0 multiply_cosine_fusion.1
  79.8 53.4 %all-reduce.14.cloned.1.call-done = (f32[4,128,256]{2,1,0:T(8,128)}, f32[4,128,8,128]{3,1,2,0:T(8,128)}) async-done(((f32[4,128,256]{2,1,0:T(8,128)}, f32[4,128,8,128]{3,1,2,0:T(8,128)}), (f32[4,128,256]{2,1,0:T(8,128)}, f32[4,128,8,128]{3,1,2,0:T(8,128)})) %all-reduce.14.cloned.1.call-update) | async-done | bytes 2621456 | tf_op jit(solution)/shard_map/psum | solution.py:86
  133.2 1.3 multiply_bitcast_fusion
  134.5 1.2 fusion.42
  135.8 3.2 fusion.12
  138.9 0.8 subtract_convert_fusion
  139.8 0.7 maximum_bitcast_fusion
  140.7 0.7 gather_fusion
  141.4 3.7 fusion.101
  145.5 0.5 fusion.102
  146.0 48.3 %pmax.7 = f32[128,1,8]{2,0,1:T(8,128)S(1)} all-reduce(f32[128,1,8]{2,0,1:T(8,128)S(1)} %maximum_bitcast_fusion.4), channel_id=1, replica_groups=mesh['seq'=16,'head'=16] {'seq'}, use_global_device_ids=true, to_apply=%region_10.0 | all-reduce | flops 1024 | bytes 8192 | tf_op jit(solution)/shard_map/pmax | solution.py:152
  194.3 0.6 gather_fusion.1
  194.9 2.9 fusion.5
  198.4 0.7 fusion.65
  199.1 1.3 fusion.21
  200.7 14.2 %all-gather = bf16[2048,8]{0,1:T(8,128)(2,1)S(1)} all-gather(bf16[128,8]{0,1:T(8,128)(2,1)S(1)} %fusion.26), channel_id=2, replica_groups=mesh['seq'=16,'head'=16] {'seq'}, dimensions={0}, use_global_device_ids=true | all-gather | bytes 34816 | tf_op jit(solution)/shard_map/all_gather | solution.py:17
  215.0 92.7 %all-reduce.8.cloned.1.call-done = bf16[128,1,8,128]{3,0,2,1:T(8,128)(2,1)} async-done(((bf16[128,1,8,128]{3,0,2,1:T(8,128)(2,1)}), bf16[128,1,8,128]{3,0,2,1:T(8,128)(2,1)}) %all-reduce.8.cloned.1.call-update) | async-done | bytes 262160 | tf_op jit(solution)/shard_map/psum | solution.py:178
  307.6 1.2 convert_divide_fusion
  308.8 2.7 convolution_convert_fusion
  311.6 1.1 fusion.25
  312.7 92.5 %all-reduce.10.cloned.1.call-done = bf16[4,128,128]{2,1,0:T(8,128)(2,1)} async-done(((bf16[4,128,128]{2,1,0:T(8,128)(2,1)}), bf16[4,128,128]{2,1,0:T(8,128)(2,1)}) %all-reduce.10.cloned.1.call-update) | async-done | bytes 131088 | tf_op jit(solution)/shard_map/psum | solution.py:193
  405.2 1.6 fusion.47
  407.1 40.6 %all-gather.3.cloned.1.call-done = bf16[4,128,2048]{2,1,0:T(8,128)(2,1)} async-done(((bf16[4,128,128]{2,1,0:T(8,128)(2,1)}), bf16[4,128,2048]{2,1,0:T(8,128)(2,1)}) %all-gather.3.cloned.1.call-update) | async-done | bytes 2097168 | tf_op jit(solution)/shard_map/all_gather | solution.py:195
  447.7 2.2 fusion.2
  450.0 0.5 fusion.4
  450.5 1.3 copy-done.2
  451.9 0.7 fusion.85
  452.6 7.3 %select_reduce_fusion.1 = f32[4,128,2]{2,1,0:T(8,128)S(1)} fusion(f32[4,128,8]{2,1,0:T(8,128)S(1)} %fusion.85, s32[4,128,2]{2,1,0:T(8,128)S(1)} %copy.126), kind=kLoop, calls=%fused_computation.44 | loop fusion | flops 23552 | bytes 24576 | tf_op jit(solution)/shard_map/reduce_sum | solution.py:203
  460.1 1.4 select_reduce_fusion
  461.7 3.5 fusion.104
  465.2 4.1 multiply_convert_fusion
  469.4 3.1 copy.133
  472.5 1.7 copy.166
  474.3 0.6 copy-done.17
  474.9 0.6 dynamic-slice
  476.2 56.6 %reduce-scatter.5.cloned.1.call-done = bf16[128,512]{1,0:T(8,128)(2,1)} async-done(((bf16[2048,512]{1,0:T(8,128)(2,1)}), bf16[128,512]{1,0:T(8,128)(2,1)}) %reduce-scatter.5.cloned.1.call-update) | async-done | bytes 131088
  532.9 0.9 reshape.454
  533.8 0.8 copy.134
  534.9 0.6 copy.129
  535.5 91.0 %all-reduce.12.cloned.1.call-done = bf16[4,128,128]{2,1,0:T(8,128)(2,1)} async-done(((bf16[4,128,128]{2,1,0:T(8,128)(2,1)}), bf16[4,128,128]{2,1,0:T(8,128)(2,1)}) %all-reduce.12.cloned.1.call-update) | async-done | bytes 131088
  626.5 1.3 add_convert_fusion.1
  (85 shorter events, 4.1 us)
Async XLA Ops:
  7.2 458.1 %copy-start = (bf16[176,2048]{1,0:T(8,128)(2,1)S(1)}, bf16[176,2048]{1,0:T(8,128)(2,1)}, u32[]{:S(2)}) copy-start(bf16[176,2048]{1,0:T(8,128)(2,1)} %param.26) | copy-start | bytes 2162692
  7.2 126.0 %all-reduce.14.cloned.1.call-start = ((), (), s32[]{:S(2)}) async-start(), calls=%async_computation.6 | async-start | bytes 5242880 | tf_op jit(solution)/shard_map/psum | solution.py:86
  10.4 2.8 copy-start.4
  10.4 3.0 copy-start.7
  10.4 8.7 %copy-start.11 = (f32[128]{0:T(128)S(1)}, f32[128]{0:T(128)}, u32[]{:S(2)}) copy-start(f32[128]{0:T(128)} %param.17) | copy-start | bytes 1540
  10.4 8.7 %copy-start.16 = (bf16[128,8]{0,1:T(8,128)(2,1)S(1)}, bf16[128,8]{0,1:T(8,128)(2,1)}, u32[]{:S(2)}) copy-start(bf16[128,8]{0,1:T(8,128)(2,1)} %param.18) | copy-start | bytes 6148
  13.1 57.1 %copy-start.12 = (s32[128]{0:T(128)S(1)}, s32[128]{0:T(128)}, u32[]{:S(2)}) copy-start(s32[128]{0:T(128)} %param.31) | copy-start | bytes 1540
  13.1 57.1 %copy-start.9 = (s32[4,128,2]{1,2,0:T(2,128)S(1)}, s32[4,128,2]{1,2,0:T(2,128)}, u32[]{:S(2)}) copy-start(s32[4,128,2]{1,2,0:T(2,128)} %param.29) | copy-start | bytes 12292
  13.2 294.5 %all-reduce.8.cloned.1.call-start = ((), (), s32[]{:S(2)}) async-start(), calls=%async_computation.1 | async-start | bytes 524288 | tf_op jit(solution)/shard_map/psum | solution.py:178
  133.2 2.6 copy-start.13
  135.7 9.7 %copy-start.5 = (bf16[4,128,1,64]{3,1,0,2:T(8,128)(2,1)}, bf16[4,128,1,64]{3,1,0,2:T(8,128)(2,1)S(1)}, u32[]{:S(2)}) copy-start(bf16[4,128,1,64]{3,1,0,2:T(8,128)(2,1)S(1)} %get-tuple-element.26) | copy-start | bytes 196612
  200.4 204.9 %all-reduce.10.cloned.1.call-start = ((), (), s32[]{:S(2)}) async-start(), calls=%async_computation.2 | async-start | bytes 262144 | tf_op jit(solution)/shard_map/psum | solution.py:193
  308.8 2.7 copy-start.14
  311.5 95.4 %copy-start.10 = (s32[4,128,2]{1,2,0:T(2,128)S(1)}, s32[4,128,2]{1,2,0:T(2,128)}, u32[]{:S(2)}) copy-start(s32[4,128,2]{1,2,0:T(2,128)} %param.30) | copy-start | bytes 12292
  311.6 138.4 %copy-start.8 = (f32[2048]{0:T(1024)S(1)}, f32[2048]{0:T(1024)}, u32[]{:S(2)}) copy-start(f32[2048]{0:T(1024)} %param.22) | copy-start | bytes 24580
  312.7 135.0 %all-gather.3.cloned.1.call-start = ((), (), s32[]{:S(2)}) async-start(), calls=%async_computation.3 | async-start | bytes 2228224 | tf_op jit(solution)/shard_map/all_gather | solution.py:195
  406.8 126.0 %reduce-scatter.5.cloned.1.call-start = ((), (), s32[]{:S(2)}) async-start(), calls=%async_computation.4 | async-start | bytes 2228224
  447.7 2.2 copy-start.1
  450.0 1.9 copy-start.15
  450.5 1.4 copy-start.2
  461.7 3.5 copy-start.3
  474.2 0.7 copy-start.17
  474.2 60.4 %copy-start.6 = (bf16[4,128,1,64]{3,1,0,2:T(8,128)(2,1)S(1)}, bf16[4,128,1,64]{3,1,0,2:T(8,128)(2,1)}, u32[]{:S(2)}) copy-start(bf16[4,128,1,64]{3,1,0,2:T(8,128)(2,1)} %copy-done.5) | copy-start | bytes 196612
  474.2 152.2 %all-reduce.12.cloned.1.call-start = ((), (), s32[]{:S(2)}) async-start(), calls=%async_computation.5 | async-start | bytes 262144
Sparse Core Ops, SparseCore 0:
  13.3 119.8 all-reduce.13
  200.5 107.0 all-reduce.7
  312.8 92.3 all-reduce.9
  407.0 40.6 all-gather.2
  474.3 58.4 reduce-scatter.4
  535.9 90.5 all-reduce.11
